TPU v7x, 512 devices: a whole 4x4x16 slice. The times are simulated.
512 devices in a mesh: row: 32 (over z_lo, x), col: 16 (over y, z_hi, core).
Axes of the slice: x: 4, y: 4, z: 16 (z_hi: 2, z_lo: 8; z = z_hi * 8 + z_lo), core: 2. Of those that a mesh axis runs over, the one named last changes fastest.
Arguments:
- anc_inv: bfloat16 [16384, 16384], P('row', 'col'), may hold values from -0.0546875 to 0.0546875
- panel: bfloat16 [1, 12288, 2048], P(None, 'col', 'row'), may hold values from -6 to 6
- structure: int32 [1, 96], replicated, may hold values from 0 to 127, as said below
Outputs:
- off_inv: float32 [1, 16384, 2048], P(None, 'row', 'col')
Inputs may be any that keep to these rules, and one draw needn't show every extreme that they name: Each structure[s] holds 96 distinct ancestor block indices, in the order in which the panel stores its row blocks (not sorted); each group of 8 consecutive ancestor blocks holds 5 to 7 of them, and some group of each supernode holds exactly 7.
All inputs are finite; a program needn't handle non-finite values.
Results may differ from a plain program's by a relative error of at most 0.0003.
Values may be sent and summed in bfloat16 or wider, within the bound.
No kernel may reach another device: no remote copies, remote signals or barrier semaphores. Data moves between devices by JAX's collectives and lax.ppermute only.
A program may use at most 64 MiB of HBM per device.

v0:
```python
import jax
import jax.numpy as jnp
from jax import lax
from jax.sharding import Mesh, PartitionSpec as P

BS = 128
SBLK = 96
ROW = ("zl", "x")
COL = ("y", "zh", "c")


def body(anc_inv, panel, structure):
    col_index = lax.axis_index(COL)
    row_index = lax.axis_index(ROW)
    local_rows, local_cols = anc_inv.shape
    group_blocks = local_cols // BS
    local_width = panel.shape[2]
    gathered = lax.all_gather(panel, COL, axis=1, tiled=True)
    own_blocks = row_index * (local_rows // BS) + jnp.arange(local_rows // BS, dtype=jnp.int32)
    block_ids = jnp.arange(group_blocks, dtype=jnp.int32)
    blocks_of = structure[0]
    compact = gathered[0].reshape(SBLK, BS * local_width)
    local_block = blocks_of - col_index * group_blocks
    picker = (local_block[None, :] == block_ids[:, None]).astype(jnp.bfloat16)
    picked = (
        jnp.dot(picker, compact, preferred_element_type=jnp.float32)
        .astype(jnp.bfloat16)
        .reshape(group_blocks * BS, local_width)
    )
    partial_value = jnp.dot(
        anc_inv,
        lax.all_gather(lax.all_gather(picked, "x", axis=1, tiled=True), "zl", axis=1, tiled=True),
        preferred_element_type=jnp.float32,
    )
    summed = lax.psum_scatter(partial_value, COL, scatter_dimension=1, tiled=True)
    member = jnp.any(blocks_of[None, :] == own_blocks[:, None], axis=1)
    row_mask = jnp.repeat(member, BS)
    results = [jnp.where(row_mask[:, None], -summed, jnp.zeros_like(summed))]
    return jnp.stack(results)


def solution(mesh):
    rows, cols = (mesh.shape["row"], mesh.shape["col"])
    fine = Mesh(mesh.devices.reshape(rows // 4, 4, cols // 4, 2, 2), ("zl", "x", "y", "zh", "c"))
    in_specs = (P(ROW, COL), P(None, COL, ROW), P())
    out_specs = P(None, ROW, COL)
    return jax.shard_map(body, mesh=fine, in_specs=in_specs, out_specs=out_specs, check_vma=False)
```

profile of v0, /device:TPU:2, one launch (start us, length us, event | category | flops | bytes accessed | tf_op | source)
XLA Modules:
  0.0 381.6 jit_solution(18023949575931893657)
XLA Ops:
  6.5 0.0 copy-start
  6.5 0.0 all-gather.3.cloned.1.call-start
  6.5 0.7 all-gather.3.cloned.1.call-update
  7.3 0.0 all-gather.5.cloned.1.call-start
  7.3 0.7 subtract_bitcast_fusion
  8.0 92.1 %all-gather.3.cloned.1.call-done = bf16[1,12288,64]{1,2,0:T(8,128)(2,1)} async-done(((bf16[1,768,64]{1,2,0:T(8,128)(2,1)}), bf16[1,12288,64]{1,2,0:T(8,128)(2,1)}) %all-gather.3.cloned.1.call-update) | async-done | bytes 1572880 | tf_op jit(solution)/shard_map/all_gather | solution.py:18
  100.1 4.1 %copy.10 = bf16[1,12288,64]{2,1,0:T(8,128)(2,1)} copy(bf16[1,12288,64]{1,2,0:T(8,128)(2,1)} %all-gather.3.cloned.1.call-done) | data formatting | bytes 3145728 | tf_op jit(solution)/shard_map/all_gather | solution.py:18
  104.2 4.3 %reshape_squeeze.3 = bf16[96,8192]{1,0:T(8,128)(2,1)S(1)} reshape(bf16[1,12288,64]{2,1,0:T(8,128)(2,1)} %copy.10) | data formatting | bytes 3145728 | tf_op jit(solution)/shard_map/reshape;squeeze | solution.py:22
  108.4 0.3 convolution_convert_fusion
  108.7 0.3 reshape.8
  109.0 0.1 copy.11
  109.1 13.8 %all_gather.10 = bf16[1024,256]{0,1:T(8,128)(2,1)} all-gather(bf16[1024,64]{0,1:T(8,128)(2,1)S(1)} %copy.11), channel_id=1, replica_groups=mesh['zl'=8,'x'=4,'y'=4,'zh'=2,'c'=2] {'x'}, dimensions={1}, use_global_device_ids=true | all-gather | bytes 655360 | tf_op jit(solution)/shard_map/all_gather | solution.py:32
  123.0 0.0 all-gather.5.cloned.1.call-update
  123.0 0.0 reduce-scatter.2.cloned.1.call-start
  123.0 95.2 %all-gather.5.cloned.1.call-done = bf16[1024,2048]{0,1:T(8,128)(2,1)} async-done(((bf16[1024,256]{0,1:T(8,128)(2,1)}), bf16[1024,2048]{0,1:T(8,128)(2,1)}) %all-gather.5.cloned.1.call-update) | async-done | bytes 4194320 | tf_op jit(solution)/shard_map/all_gather | solution.py:32
  218.2 0.0 copy-done
  218.2 6.5 %convolution_bitcast_fusion = f32[512,2048]{0,1:T(8,128)} fusion(bf16[1024,2048]{0,1:T(8,128)(2,1)} %all-gather.5.cloned.1.call-done, bf16[512,1024]{1,0:T(8,128)(2,1)S(1)} %copy-done), kind=kOutput, calls=%fused_computation.1 | convolution fusion | flops 2147483648 | bytes 9437184 | tf_op jit(solution)/shard_map/dot_general | solution.py:30
  224.8 0.0 reduce-scatter.2.cloned.1.call-update
  224.8 0.6 copy-done.1
  225.4 0.2 compare_reduce_fusion
  225.6 0.1 broadcast_bitcast_fusion
  225.7 147.5 %reduce-scatter.2.cloned.1.call-done = f32[512,128]{0,1:T(8,128)} async-done(((f32[512,2048]{0,1:T(8,128)}), f32[512,128]{0,1:T(8,128)}) %reduce-scatter.2.cloned.1.call-update) | async-done | bytes 262160 | tf_op jit(solution)/shard_map/reduce_scatter | solution.py:35
  373.2 1.0 select_bitcast_fusion
  374.2 0.8 copy.12
  (2 shorter events, 0.0 us)
Async XLA Ops:
  6.5 211.7 %copy-start = (bf16[512,1024]{1,0:T(8,128)(2,1)S(1)}, bf16[512,1024]{1,0:T(8,128)(2,1)}, u32[]{:S(2)}) copy-start(bf16[512,1024]{1,0:T(8,128)(2,1)} %param.3) | copy-start | bytes 3145732
  6.5 93.5 %all-gather.3.cloned.1.call-start = ((), (), s32[]{:S(2)}) async-start(), calls=%async_computation.1 | async-start | bytes 1671168 | tf_op jit(solution)/shard_map/all_gather | solution.py:18
  7.3 210.9 %all-gather.5.cloned.1.call-start = ((), (), s32[]{:S(2)}) async-start(), calls=%async_computation.2 | async-start | bytes 4718592 | tf_op jit(solution)/shard_map/all_gather | solution.py:32
  123.0 250.2 %reduce-scatter.2.cloned.1.call-start = ((), (), s32[]{:S(2)}) async-start(), calls=%async_computation.3 | async-start | bytes 4456448 | tf_op jit(solution)/shard_map/reduce_scatter | solution.py:35
  224.8 0.7 copy-start.1
Sparse Core Ops, SparseCore 0:
  10.6 89.3 all-gather.2
  123.1 95.0 all-gather.4
  224.9 148.2 reduce-scatter.1
where the time goes:
time: 382 us
  waiting for transfers between devices  336 us (88%)
  blocking collectives  13.8 us (4%)
  between operations  13.2 us (3%)
  local copies, waits for them, and re-layouts  10.3 us (3%)
  matrix products  6.86 us (2%)
    reduce_scatter x1, waiting for transfers between devices, body(): lax.psum_scatter(partial_value, COL, scatter_dimension=1, tiled=True)  148 us
    all_gather x1, waiting for transfers between devices, body(): lax.all_gather(lax.all_gather(picked, 'x', axis=1, tiled=True), 'zl', axi...  95.2 us
    all_gather x1, waiting for transfers between devices, body(): gathered = lax.all_gather(panel, COL, axis=1, tiled=True)  92.1 us
    all_gather x1, blocking collectives, body(): lax.all_gather(picked, 'x', axis=1, tiled=True)  13.8 us
  transfers between devices with their start and end apart: 3, of which 3 were waited for; matrix products, arithmetic and copies ran while one was open for 0% of the time, Pallas kernels for 0%

commit v1 on v0

--- a/solution.py
+++ b/solution.py
@@ -15,7 +15,9 @@
     local_rows, local_cols = anc_inv.shape
     group_blocks = local_cols // BS
     local_width = panel.shape[2]
-    gathered = lax.all_gather(panel, COL, axis=1, tiled=True)
+    gathered = jnp.concatenate(
+        lax.all_to_all(jnp.stack([panel] * lax.axis_size(COL)), COL, 0, 0), axis=1
+    )
     own_blocks = row_index * (local_rows // BS) + jnp.arange(local_rows // BS, dtype=jnp.int32)
     block_ids = jnp.arange(group_blocks, dtype=jnp.int32)
     blocks_of = structure[0]

time: 382 us -> 390 us (1.021)
  starting transfers between devices: 0.08 us -> 17.9 us
  waiting for transfers between devices: 336 us -> 325 us
    all_gather x1 -> x0, waiting for transfers between devices: 92.1 us -> none  [body(): gathered = lax.all_gather(panel, COL, axis=1, tiled=True)]
    all_gather x1, waiting for transfers between devices: 95.2 us -> 137 us  [body(): lax.all_gather(lax.all_gather(picked, 'x', axis=1, tiled=True), 'zl', axi...]
    all_to_all x0 -> x1, waiting for transfers between devices: none -> 40.8 us  [body(): lax.all_to_all(jnp.stack([panel] * lax.axis_size(COL)), COL, 0, 0)]
    all_to_all x0 -> x1, starting transfers between devices: none -> 17.8 us  [body(): lax.all_to_all(jnp.stack([panel] * lax.axis_size(COL)), COL, 0, 0)]
    all_gather x1 -> x0, local copies, waits for them, and re-layouts: 4.12 us -> none  [body(): gathered = lax.all_gather(panel, COL, axis=1, tiled=True)]
where the time goes in v1:
time: 390 us
  waiting for transfers between devices  325 us (83%)
  starting transfers between devices  17.9 us (5%)
  blocking collectives  14.3 us (4%)
  between operations  13.5 us (3%)
  local copies, waits for them, and re-layouts  10.7 us (3%)
  matrix products  6.84 us (2%)
    reduce_scatter x1, waiting for transfers between devices, body(): lax.psum_scatter(partial_value, COL, scatter_dimension=1, tiled=True)  148 us
    all_gather x1, waiting for transfers between devices, body(): lax.all_gather(lax.all_gather(picked, 'x', axis=1, tiled=True), 'zl', axi...  137 us
    all_to_all x1, waiting for transfers between devices, body(): lax.all_to_all(jnp.stack([panel] * lax.axis_size(COL)), COL, 0, 0)  40.8 us
    all_to_all x1, starting transfers between devices, body(): lax.all_to_all(jnp.stack([panel] * lax.axis_size(COL)), COL, 0, 0)  17.8 us
    all_gather x1, blocking collectives, body(): lax.all_gather(picked, 'x', axis=1, tiled=True)  14.3 us
  transfers between devices with their start and end apart: 3, of which 3 were waited for; matrix products, arithmetic and copies ran while one was open for 0% of the time, Pallas kernels for 0%

profile of v1, /device:TPU:2, one launch (start us, length us, event | category | flops | bytes accessed | tf_op | source)
XLA Modules:
  0.0 389.7 jit_solution(8852910109037708757)
XLA Ops:
  6.5 0.0 copy-start
  6.5 0.0 copy-start.1
  6.5 2.3 stack.4
  8.9 17.8 %all-to-all-start = ((bf16[16,1,768,64]{2,3,1,0:T(8,128)(2,1)}), bf16[16,1,768,64]{2,3,1,0:T(8,128)(2,1)S(1)}, u32[]{:S(2)}, u32[]{:S(2)}) async-start(bf16[16,1,768,64]{2,3,1,0:T(8,128)(2,1)} %stack.4), calls=%async_computation | async-start | bytes 3145728 | tf_op jit(solution)/shard_map/all_to_all | solution.py:19
  26.7 0.0 all-gather.2.cloned.1.call-start
  26.7 0.0 copy-done.1
  26.8 40.8 %all-to-all-done = bf16[16,1,768,64]{2,3,1,0:T(8,128)(2,1)S(1)} async-done(((bf16[16,1,768,64]{2,3,1,0:T(8,128)(2,1)}), bf16[16,1,768,64]{2,3,1,0:T(8,128)(2,1)S(1)}, u32[]{:S(2)}, u32[]{:S(2)}) %all-to-all-start) | async-done | bytes 1572896 | tf_op jit(solution)/shard_map/all_to_all | solution.py:19
  67.5 2.8 copy.11
  70.4 4.3 %reshape_squeeze_reshape.3 = bf16[96,8192]{1,0:T(8,128)(2,1)S(1)} reshape(bf16[16,1,768,64]{3,2,0,1:T(8,128)(2,1)} %copy.11) | data formatting | bytes 3145728 | tf_op jit(solution)/shard_map/reshape;squeeze;reshape | solution.py:24
  74.6 0.3 convolution_convert_fusion
  74.9 0.3 reshape.11
  75.2 0.1 copy.12
  75.3 14.3 %all_gather.6 = bf16[1024,256]{0,1:T(8,128)(2,1)} all-gather(bf16[1024,64]{0,1:T(8,128)(2,1)S(1)} %copy.12), channel_id=1, replica_groups=mesh['zl'=8,'x'=4,'y'=4,'zh'=2,'c'=2] {'x'}, dimensions={1}, use_global_device_ids=true | all-gather | bytes 655360 | tf_op jit(solution)/shard_map/all_gather | solution.py:34
  89.6 0.0 all-gather.2.cloned.1.call-update
  89.6 0.0 reduce-scatter.2.cloned.1.call-start
  89.7 136.7 %all-gather.2.cloned.1.call-done = bf16[1024,2048]{0,1:T(8,128)(2,1)} async-done(((bf16[1024,256]{0,1:T(8,128)(2,1)}), bf16[1024,2048]{0,1:T(8,128)(2,1)}) %all-gather.2.cloned.1.call-update) | async-done | bytes 4194320 | tf_op jit(solution)/shard_map/all_gather | solution.py:34
  226.4 0.0 copy-done
  226.4 6.5 %convolution_bitcast_fusion = f32[512,2048]{0,1:T(8,128)} fusion(bf16[1024,2048]{0,1:T(8,128)(2,1)} %all-gather.2.cloned.1.call-done, bf16[512,1024]{1,0:T(8,128)(2,1)S(1)} %copy-done), kind=kOutput, calls=%fused_computation.1 | convolution fusion | flops 2147483648 | bytes 9437184 | tf_op jit(solution)/shard_map/dot_general | solution.py:32
  232.9 0.0 reduce-scatter.2.cloned.1.call-update
  232.9 0.2 compare_reduce_fusion
  233.1 0.1 broadcast_bitcast_fusion
  233.2 147.8 %reduce-scatter.2.cloned.1.call-done = f32[512,128]{0,1:T(8,128)} async-done(((f32[512,2048]{0,1:T(8,128)}), f32[512,128]{0,1:T(8,128)}) %reduce-scatter.2.cloned.1.call-update) | async-done | bytes 262160 | tf_op jit(solution)/shard_map/reduce_scatter | solution.py:37
  381.0 1.0 select_bitcast_fusion
  382.0 0.8 copy.13
  (2 shorter events, 0.0 us)
Async XLA Ops:
  6.5 219.8 %copy-start = (bf16[512,1024]{1,0:T(8,128)(2,1)S(1)}, bf16[512,1024]{1,0:T(8,128)(2,1)}, u32[]{:S(2)}) copy-start(bf16[512,1024]{1,0:T(8,128)(2,1)} %param.3) | copy-start | bytes 3145732
  6.5 20.2 %copy-start.1 = (s32[1,96]{1,0:T(1,128)S(1)}, s32[1,96]{1,0:T(1,128)}, u32[]{:S(2)}) copy-start(s32[1,96]{1,0:T(1,128)} %param.5) | copy-start | bytes 1156
  8.9 58.7 %all-to-all-start = ((bf16[16,1,768,64]{2,3,1,0:T(8,128)(2,1)}), bf16[16,1,768,64]{2,3,1,0:T(8,128)(2,1)S(1)}, u32[]{:S(2)}, u32[]{:S(2)}) async-start(bf16[16,1,768,64]{2,3,1,0:T(8,128)(2,1)} %stack.4), calls=%async_computation | async-start | bytes 3145728 | tf_op jit(solution)/shard_map/all_to_all | solution.py:19
  26.7 199.7 %all-gather.2.cloned.1.call-start = ((), (), s32[]{:S(2)}) async-start(), calls=%async_computation.2 | async-start | bytes 4718592 | tf_op jit(solution)/shard_map/all_gather | solution.py:34
  89.6 291.4 %reduce-scatter.2.cloned.1.call-start = ((), (), s32[]{:S(2)}) async-start(), calls=%async_computation.3 | async-start | bytes 4456448 | tf_op jit(solution)/shard_map/reduce_scatter | solution.py:37
Sparse Core Ops, SparseCore 0:
  89.7 136.5 all-gather.1
  233.0 147.9 reduce-scatter.1
